TPU v7x, 512 devices: a whole 4x8x8 slice. The times are simulated.
512 devices in a mesh: ctx: 32 (over y_lo, z, core), tp: 16 (over x, y_hi).
Axes of the slice: x: 4, y: 8 (y_hi: 4, y_lo: 2; y = y_hi * 2 + y_lo), z: 8, core: 2. Of those that a mesh axis runs over, the one named last changes fastest.
Arguments:
- query: bfloat16 [8192, 4096], P('ctx', 'tp'), may hold values from 0.049804688 to 2
- key_feat: bfloat16 [8192, 4096], P('ctx', 'tp'), may hold values from 0.049804688 to 2
- value: bfloat16 [8192, 4096], P('ctx', 'tp'), may hold values from -36 to 36
- grad_out: bfloat16 [8192, 4096], P('ctx', 'tp'), may hold values from -6 to 6
- w_out: bfloat16 [4096, 4096], P('tp', 'ctx'), may hold values from -0.09375 to 0.09375
Outputs:
- grad_query: bfloat16 [8192, 4096], P('ctx', 'tp')
- grad_key: bfloat16 [8192, 4096], P('ctx', 'tp')
- grad_value: bfloat16 [8192, 4096], P('ctx', 'tp')
All inputs are finite; a program needn't handle non-finite values.
Results may differ from a plain program's by a relative error of at most 0.0059.
Values may be sent and summed in bfloat16 or wider, within the bound.
No kernel may reach another device: no remote copies, remote signals or barrier semaphores. Data moves between devices by JAX's collectives and lax.ppermute only.
A program may use at most 64 MiB of HBM per device.

v0:
```python
import jax
import jax.numpy as jnp
from jax import lax
from jax.sharding import PartitionSpec as P

E = 128
epsilon = 1e-06
highest = lax.Precision.HIGHEST


def prefix(value, axis, join, neutral, backward):
    count, mine = (lax.axis_size(axis), lax.axis_index(axis))
    pieces = lax.all_gather(value, axis)
    if backward:
        pieces = pieces[::-1]
        mine = count - 1 - mine
    subtotal = jnp.full_like(value, 0) + jnp.asarray(neutral, value.dtype)

    def lap(position, subtotal):
        longer = join(subtotal, pieces[position])
        return jnp.where(position < mine, longer, subtotal)

    return lax.fori_loop(0, count - 1, lap, subtotal)


def add_states(earlier, later):
    return earlier + later


def local(query, key_feat, value, grad_out, w_out):
    tok_rows = query.shape[0]
    feat_width = query.shape[1]
    head_count = feat_width // E
    full_rows = lax.all_gather(grad_out, "tp", axis=1, tiled=True)
    grad_z = lax.dot_general(
        full_rows,
        lax.all_gather(w_out, "ctx", axis=1, tiled=True),
        (((1,), (1,)), ((), ())),
        preferred_element_type=jnp.float32,
    )
    query_heads = query.reshape(tok_rows, head_count, E)
    key_heads = key_feat.reshape(tok_rows, head_count, E)
    value_heads = value.reshape(tok_rows, head_count, E)
    gradz_heads = grad_z.reshape(tok_rows, head_count, E)
    query_wide = query_heads.astype(jnp.float32)
    key_wide = key_heads.astype(jnp.float32)
    value_wide = value_heads.astype(jnp.float32)
    causal = (
        lax.broadcasted_iota(jnp.int32, (tok_rows, tok_rows), 0)
        >= lax.broadcasted_iota(jnp.int32, (tok_rows, tok_rows), 1)
    )[None]
    scores = jnp.einsum("thd,shd->hts", query_heads, key_heads, preferred_element_type=jnp.float32)
    weights = jnp.where(causal, scores, 0.0)
    local_state = jnp.einsum(
        "shd,she->hde", key_heads, value_heads, preferred_element_type=jnp.float32
    )
    empty_state = jnp.zeros_like(local_state)
    state_in = prefix(local_state, "ctx", add_states, empty_state, False)
    attended = jnp.einsum("hts,she->the", weights, value_wide, precision=highest)
    attended = attended + jnp.einsum("thd,hde->the", query_wide, state_in, precision=highest)
    inv_rms = lax.rsqrt(jnp.mean(attended * attended, axis=-1, keepdims=True) + epsilon)
    normed = attended * inv_rms
    grad_att = (
        inv_rms * (gradz_heads - normed * jnp.mean(gradz_heads * normed, axis=-1, keepdims=True))
    ).astype(jnp.bfloat16)
    grad_wide = grad_att.astype(jnp.float32)
    grad_weights = jnp.where(
        causal,
        jnp.einsum("the,she->hts", grad_att, value_heads, preferred_element_type=jnp.float32),
        0.0,
    )
    grad_query = jnp.einsum("hts,shd->thd", grad_weights, key_wide, precision=highest)
    grad_query = grad_query + jnp.einsum("the,hde->thd", grad_wide, state_in, precision=highest)
    local_adjoint = jnp.einsum(
        "thd,the->hde", query_heads, grad_att, preferred_element_type=jnp.float32
    )
    adjoint = prefix(local_adjoint, "ctx", add_states, empty_state, True)
    grad_key = jnp.einsum("hts,thd->shd", grad_weights, query_wide, precision=highest)
    grad_key = grad_key + jnp.einsum("she,hde->shd", value_wide, adjoint, precision=highest)
    grad_value = jnp.einsum("hts,the->she", weights, grad_wide, precision=highest)
    grad_value = grad_value + jnp.einsum("shd,hde->she", key_wide, adjoint, precision=highest)
    return (
        grad_query.reshape(tok_rows, feat_width).astype(jnp.bfloat16),
        grad_key.reshape(tok_rows, feat_width).astype(jnp.bfloat16),
        grad_value.reshape(tok_rows, feat_width).astype(jnp.bfloat16),
    )


def solution(mesh):
    return jax.shard_map(
        local,
        mesh=mesh,
        in_specs=(P("ctx", "tp"), P("ctx", "tp"), P("ctx", "tp"), P("ctx", "tp"), P("tp", "ctx")),
        out_specs=(P("ctx", "tp"), P("ctx", "tp"), P("ctx", "tp")),
        check_vma=False,
    )
```

profile of v0, /device:TPU:1, one launch (start us, length us, event | category | flops | bytes accessed | tf_op | source)
XLA Modules:
  0.0 341.3 jit_solution(11616398118935155709)
XLA Ops:
  7.2 1.1 copy.95
  10.8 1.2 convolution_select_fusion.1
  12.0 74.3 %all-gather.11.cloned.1.call-done = f32[64,128,128]{2,1,0:T(8,128)} async-done(((f32[2,128,128]{2,1,0:T(8,128)}), f32[64,128,128]{2,1,0:T(8,128)}) %all-gather.11.cloned.1.call-update) | async-done | bytes 4194320 | tf_op jit(solution)/shard_map/all_gather | solution.py:13
  86.3 30.2 %while.28 = (s32[]{:T(128)}, f32[2,128,128]{2,1,0:T(8,128)S(1)}, s32[]{:T(128)}, f32[32,2,128,128]{3,2,1,0:T(8,128)}, s32[]{:T(128)}, /*index=5*/s32[]{:T(128)}) while((s32[]{:T(128)}, f32[2,128,128]{2,1,0:T(8,128)S(1)}, s32[]{:T(128)}, f32[32,2,128,128]{3,2,1,0:T(8,128)}, s32[]{:T(128)}, /*index=5*/s32[]{:T(128)}) %tuple.81), condition=%wide.region_1.2_spmd.clone, body=%wide.region_0.1_spmd.clone.sunk | while | flops 98308 | bytes 393317 | solution.py:23
  87.2 0.9 add_select_fusion.4
  88.2 0.9 add_select_fusion.4
  89.2 0.9 add_select_fusion.4
  90.2 0.9 add_select_fusion.4
  91.1 0.9 add_select_fusion.4
  92.1 0.9 add_select_fusion.4
  93.1 0.9 add_select_fusion.4
  94.1 0.9 add_select_fusion.4
  95.0 0.9 add_select_fusion.4
  96.0 0.9 add_select_fusion.4
  97.0 0.9 add_select_fusion.4
  98.0 0.9 add_select_fusion.4
  98.9 0.9 add_select_fusion.4
  99.9 0.9 add_select_fusion.4
  100.9 0.9 add_select_fusion.4
  101.8 0.9 add_select_fusion.4
  102.8 1.0 add_select_fusion.4
  103.8 1.0 add_select_fusion.4
  104.8 0.9 add_select_fusion.4
  105.7 0.9 add_select_fusion.4
  106.7 0.9 add_select_fusion.4
  107.7 0.9 add_select_fusion.4
  108.7 0.9 add_select_fusion.4
  109.6 1.0 add_select_fusion.4
  110.6 1.0 add_select_fusion.4
  111.6 0.9 add_select_fusion.4
  112.6 0.9 add_select_fusion.4
  113.5 0.9 add_select_fusion.4
  114.5 1.0 add_select_fusion.4
  115.5 0.9 add_select_fusion.4
  117.3 36.0 %all-gather.7.cloned.1.call-done = bf16[256,4096]{1,0:T(8,128)(2,1)} async-done(((bf16[256,256]{1,0:T(8,128)(2,1)}), bf16[256,4096]{1,0:T(8,128)(2,1)}) %all-gather.7.cloned.1.call-update) | async-done | bytes 2097168 | tf_op jit(solution)/shard_map/all_gather | solution.py:34
  153.3 72.8 %all-gather.9.cloned.1.call-done = bf16[256,4096]{1,0:T(8,128)(2,1)} async-done(((bf16[256,128]{1,0:T(8,128)(2,1)}), bf16[256,4096]{1,0:T(8,128)(2,1)}) %all-gather.9.cloned.1.call-update) | async-done | bytes 2097168 | tf_op jit(solution)/shard_map/all_gather | solution.py:37
  226.1 3.0 multiply_reduce_fusion
  232.2 65.2 %all-gather.13.cloned.1.call-done = f32[64,128,128]{2,1,0:T(8,128)} async-done(((f32[2,128,128]{2,1,0:T(8,128)}), f32[64,128,128]{2,1,0:T(8,128)}) %all-gather.13.cloned.1.call-update) | async-done | bytes 4194320 | tf_op jit(solution)/shard_map/all_gather | solution.py:13
  297.4 4.7 %rev.3 = f32[32,2,128,128]{3,2,1,0:T(8,128)} reverse(f32[32,2,128,128]{3,2,1,0:T(8,128)} %bitcast.117), dimensions={0} | reverse | bytes 8388608 | tf_op jit(solution)/shard_map/rev | solution.py:15
  302.1 30.2 %while.29 = (s32[]{:T(128)}, f32[2,128,128]{2,1,0:T(8,128)S(1)}, s32[]{:T(128)}, f32[32,2,128,128]{3,2,1,0:T(8,128)}, s32[]{:T(128)}, /*index=5*/s32[]{:T(128)}) while((s32[]{:T(128)}, f32[2,128,128]{2,1,0:T(8,128)S(1)}, s32[]{:T(128)}, f32[32,2,128,128]{3,2,1,0:T(8,128)}, s32[]{:T(128)}, /*index=5*/s32[]{:T(128)}) %tuple.70), condition=%wide.region_5.6_spmd.clone, body=%wide.region_4.5_spmd.clone.sunk | while | flops 98308 | bytes 393317 | solution.py:23
  302.1 1.0 add_select_fusion.5
  303.1 0.9 add_select_fusion.5
  304.1 0.9 add_select_fusion.5
  305.0 0.9 add_select_fusion.5
  306.0 0.9 add_select_fusion.5
  307.0 0.9 add_select_fusion.5
  307.9 0.9 add_select_fusion.5
  308.9 0.9 add_select_fusion.5
  (59 shorter events, 31.5 us)
Async XLA Ops:
  7.2 1.1 copy-start
  7.2 109.3 %copy-start.1 = (bf16[256,256]{1,0:T(8,128)(2,1)S(1)}, bf16[256,256]{1,0:T(8,128)(2,1)}, u32[]{:S(2)}) copy-start(bf16[256,256]{1,0:T(8,128)(2,1)} %param.9) | copy-start | bytes 393220
  7.2 79.1 %all-gather.11.cloned.1.call-start = ((), (), s32[]{:S(2)}) async-start(), calls=%async_computation.2 | async-start | bytes 4325376 | tf_op jit(solution)/shard_map/all_gather | solution.py:13
  9.2 144.1 %all-gather.7.cloned.1.call-start = ((), (), s32[]{:S(2)}) async-start(), calls=%async_computation | async-start | bytes 2228224 | tf_op jit(solution)/shard_map/all_gather | solution.py:34
  9.9 216.1 %all-gather.9.cloned.1.call-start = ((), (), s32[]{:S(2)}) async-start(), calls=%async_computation.1 | async-start | bytes 2162688 | tf_op jit(solution)/shard_map/all_gather | solution.py:37
  10.7 286.8 %all-gather.13.cloned.1.call-start = ((), (), s32[]{:S(2)}) async-start(), calls=%async_computation.3 | async-start | bytes 4325376 | tf_op jit(solution)/shard_map/all_gather | solution.py:13
  302.1 30.5 %copy-start.2 = (bf16[256,256]{1,0:T(8,128)(2,1)S(1)}, bf16[256,256]{1,0:T(8,128)(2,1)}, u32[]{:S(2)}) copy-start(bf16[256,256]{1,0:T(8,128)(2,1)} %param.10) | copy-start | bytes 393220
Sparse Core Ops, SparseCore 0:
  10.7 75.5 all-gather.10
  89.3 63.9 all-gather.6
  155.3 70.6 all-gather.8
  230.2 67.1 all-gather.12
where the time goes:
time: 343 us; the launch traced here: 341 us
  waiting for transfers between devices  250 us (73%)
  other arithmetic  59 us (17%)
  between operations  13.9 us (4%)
  local copies, waits for them, and re-layouts  8.78 us (3%)
  matrix products  8.2 us (2%)
    all_gather x2, waiting for transfers between devices, prefix(): pieces = lax.all_gather(value, axis)  140 us
    all_gather x1, waiting for transfers between devices, local(): lax.all_gather(w_out, 'ctx', axis=1, tiled=True)  72.8 us
    select_n x62, other arithmetic, lap(): return jnp.where(position < mine, longer, subtotal)  58.9 us
    all_gather x1, waiting for transfers between devices, local(): full_rows = lax.all_gather(grad_out, 'tp', axis=1, tiled=True)  36 us
  transfers between devices with their start and end apart: 4, of which 4 were waited for; matrix products, arithmetic and copies ran while one was open for 10% of the time, Pallas kernels for 0%

commit v1 on v0

--- a/solution.py
+++ b/solution.py
@@ -31,7 +31,9 @@
     tok_rows = query.shape[0]
     feat_width = query.shape[1]
     head_count = feat_width // E
-    full_rows = lax.all_gather(grad_out, "tp", axis=1, tiled=True)
+    full_rows = jnp.concatenate(
+        lax.all_to_all(jnp.stack([grad_out] * lax.axis_size("tp")), "tp", 0, 0), axis=1
+    )
     grad_z = lax.dot_general(
         full_rows,
         lax.all_gather(w_out, "ctx", axis=1, tiled=True),

time: 343 us -> 287 us (0.84)
  waiting for transfers between devices: 250 us -> 176 us
  starting transfers between devices: 0.16 us -> 10.5 us
  local copies, waits for them, and re-layouts: 8.78 us -> 17.2 us
    all_gather x2, waiting for transfers between devices: 140 us -> 72.6 us  [prefix(): pieces = lax.all_gather(value, axis)]
    all_to_all x0 -> x1, waiting for transfers between devices: none -> 64 us  [local(): lax.all_to_all(jnp.stack([grad_out] * lax.axis_size('tp')), 'tp', 0, 0)]
    all_gather x1 -> x0, waiting for transfers between devices: 36 us -> none  [local(): full_rows = lax.all_gather(grad_out, 'tp', axis=1, tiled=True)]
    all_gather x1, waiting for transfers between devices: 72.8 us -> 38.9 us  [local(): lax.all_gather(w_out, 'ctx', axis=1, tiled=True)]
    all_to_all x0 -> x1, starting transfers between devices: none -> 10.3 us  [local(): lax.all_to_all(jnp.stack([grad_out] * lax.axis_size('tp')), 'tp', 0, 0)]
    reshape x0 -> x2, local copies, waits for them, and re-layouts: none -> 5.43 us  [local(): jnp.concatenate(lax.all_to_all(jnp.stack([grad_out] * lax.axis_size('tp')...]
  transfers between devices with their start and end apart: 4 -> 4, of which waited for: 4 -> 4; matrix products, arithmetic and copies ran while one was open for 10% -> 14% of each run, Pallas kernels for 0% -> 0%
where the time goes in v1:
time: 287 us; the launch traced here: 286 us
  waiting for transfers between devices  176 us (61%)
  other arithmetic  59 us (21%)
  local copies, waits for them, and re-layouts  17.2 us (6%)
  between operations  13.9 us (5%)
  starting transfers between devices  10.5 us (4%)
  matrix products  7.42 us (3%)
    all_gather x2, waiting for transfers between devices, prefix(): pieces = lax.all_gather(value, axis)  72.6 us
    all_to_all x1, waiting for transfers between devices, local(): lax.all_to_all(jnp.stack([grad_out] * lax.axis_size('tp')), 'tp', 0, 0)  64 us
    select_n x62, other arithmetic, lap(): return jnp.where(position < mine, longer, subtotal)  58.9 us
    all_gather x1, waiting for transfers between devices, local(): lax.all_gather(w_out, 'ctx', axis=1, tiled=True)  38.9 us
    all_to_all x1, starting transfers between devices, local(): lax.all_to_all(jnp.stack([grad_out] * lax.axis_size('tp')), 'tp', 0, 0)  10.3 us
  transfers between devices with their start and end apart: 4, of which 4 were waited for; matrix products, arithmetic and copies ran while one was open for 14% of the time, Pallas kernels for 0%

profile of v1, /device:TPU:1, one launch (start us, length us, event | category | flops | bytes accessed | tf_op | source)
XLA Modules:
  0.0 285.6 jit_solution(11122565761470836422)
XLA Ops:
  7.2 1.0 copy.96
  9.1 2.5 stack.2
  11.6 10.3 %all-to-all-start = ((bf16[16,256,256]{2,1,0:T(8,128)(2,1)}), bf16[16,256,256]{2,1,0:T(8,128)(2,1)S(1)}, u32[]{:S(2)}, u32[]{:S(2)}) async-start(bf16[16,256,256]{2,1,0:T(8,128)(2,1)} %stack.2), calls=%async_computation | async-start | bytes 4194304 | tf_op jit(solution)/shard_map/all_to_all | solution.py:35
  23.7 64.0 %all-to-all-done = bf16[16,256,256]{2,1,0:T(8,128)(2,1)S(1)} async-done(((bf16[16,256,256]{2,1,0:T(8,128)(2,1)}), bf16[16,256,256]{2,1,0:T(8,128)(2,1)S(1)}, u32[]{:S(2)}, u32[]{:S(2)}) %all-to-all-start) | async-done | bytes 2097184 | tf_op jit(solution)/shard_map/all_to_all | solution.py:35
  87.6 2.5 copy.35
  90.2 2.9 %reshape.57 = bf16[256,4096,1]{1,0,2:T(8,128)(2,1)S(1)} reshape(bf16[256,16,256]{2,1,0:T(8,128)(2,1)} %copy.35) | data formatting | bytes 4194304 | tf_op jit(solution)/shard_map/reshape | solution.py:34
  93.1 8.1 %all-gather.8.cloned.1.call-done = f32[64,128,128]{2,1,0:T(8,128)} async-done(((f32[2,128,128]{2,1,0:T(8,128)}), f32[64,128,128]{2,1,0:T(8,128)}) %all-gather.8.cloned.1.call-update) | async-done | bytes 4194320 | tf_op jit(solution)/shard_map/all_gather | solution.py:13
  101.2 30.2 %while.28 = (s32[]{:T(128)}, f32[2,128,128]{2,1,0:T(8,128)S(1)}, s32[]{:T(128)}, f32[32,2,128,128]{3,2,1,0:T(8,128)}, s32[]{:T(128)}, /*index=5*/s32[]{:T(128)}) while((s32[]{:T(128)}, f32[2,128,128]{2,1,0:T(8,128)S(1)}, s32[]{:T(128)}, f32[32,2,128,128]{3,2,1,0:T(8,128)}, s32[]{:T(128)}, /*index=5*/s32[]{:T(128)}) %tuple.79), condition=%wide.region_1.2_spmd.clone, body=%wide.region_0.1_spmd.clone.sunk | while | flops 98308 | bytes 393317 | solution.py:23
  102.2 0.9 add_select_fusion.4
  103.2 0.9 add_select_fusion.4
  104.1 0.9 add_select_fusion.4
  105.1 0.9 add_select_fusion.4
  106.1 0.9 add_select_fusion.4
  107.1 0.9 add_select_fusion.4
  108.0 0.9 add_select_fusion.4
  109.0 0.9 add_select_fusion.4
  110.0 0.9 add_select_fusion.4
  110.9 0.9 add_select_fusion.4
  111.9 0.9 add_select_fusion.4
  112.9 0.9 add_select_fusion.4
  113.9 0.9 add_select_fusion.4
  114.8 0.9 add_select_fusion.4
  115.8 0.9 add_select_fusion.4
  116.8 0.9 add_select_fusion.4
  117.8 0.9 add_select_fusion.4
  118.7 0.9 add_select_fusion.4
  119.7 0.9 add_select_fusion.4
  120.7 0.9 add_select_fusion.4
  121.6 0.9 add_select_fusion.4
  122.6 1.0 add_select_fusion.4
  123.6 0.9 add_select_fusion.4
  124.6 0.9 add_select_fusion.4
  125.6 1.0 add_select_fusion.4
  126.6 0.9 add_select_fusion.4
  127.5 0.9 add_select_fusion.4
  128.5 0.9 add_select_fusion.4
  129.5 0.9 add_select_fusion.4
  130.4 0.9 add_select_fusion.4
  132.2 38.9 %all-gather.6.cloned.1.call-done = bf16[256,4096]{1,0:T(8,128)(2,1)} async-done(((bf16[256,128]{1,0:T(8,128)(2,1)}), bf16[256,4096]{1,0:T(8,128)(2,1)}) %all-gather.6.cloned.1.call-update) | async-done | bytes 2097168 | tf_op jit(solution)/shard_map/all_gather | solution.py:39
  171.1 2.3 multiply_reduce_fusion
  174.7 1.1 convolution_select_fusion
  177.4 64.4 %all-gather.10.cloned.1.call-done = f32[64,128,128]{2,1,0:T(8,128)} async-done(((f32[2,128,128]{2,1,0:T(8,128)}), f32[64,128,128]{2,1,0:T(8,128)}) %all-gather.10.cloned.1.call-update) | async-done | bytes 4194320 | tf_op jit(solution)/shard_map/all_gather | solution.py:13
  241.8 4.6 %rev.3 = f32[32,2,128,128]{3,2,1,0:T(8,128)} reverse(f32[32,2,128,128]{3,2,1,0:T(8,128)} %bitcast.117), dimensions={0} | reverse | bytes 8388608 | tf_op jit(solution)/shard_map/rev | solution.py:15
  246.4 30.2 %while.29 = (s32[]{:T(128)}, f32[2,128,128]{2,1,0:T(8,128)S(1)}, s32[]{:T(128)}, f32[32,2,128,128]{3,2,1,0:T(8,128)}, s32[]{:T(128)}, /*index=5*/s32[]{:T(128)}) while((s32[]{:T(128)}, f32[2,128,128]{2,1,0:T(8,128)S(1)}, s32[]{:T(128)}, f32[32,2,128,128]{3,2,1,0:T(8,128)}, s32[]{:T(128)}, /*index=5*/s32[]{:T(128)}) %tuple.70), condition=%wide.region_5.6_spmd.clone, body=%wide.region_4.5_spmd.clone.sunk | while | flops 98308 | bytes 393317 | solution.py:23
  247.4 0.9 add_select_fusion.5
  248.4 0.9 add_select_fusion.5
  249.4 0.9 add_select_fusion.5
  250.3 0.9 add_select_fusion.5
  (63 shorter events, 35.2 us)
Async XLA Ops:
  7.2 1.1 copy-start
  7.2 94.0 %all-gather.8.cloned.1.call-start = ((), (), s32[]{:S(2)}) async-start(), calls=%async_computation.2 | async-start | bytes 4325376 | tf_op jit(solution)/shard_map/all_gather | solution.py:13
  11.6 11.8 %copy-start.1 = (bf16[256,256]{1,0:T(8,128)(2,1)S(1)}, bf16[256,256]{1,0:T(8,128)(2,1)}, u32[]{:S(2)}) copy-start(bf16[256,256]{1,0:T(8,128)(2,1)} %param.9) | copy-start | bytes 393220
  11.6 11.8 %copy-start.2 = (bf16[256,256]{1,0:T(8,128)(2,1)S(1)}, bf16[256,256]{1,0:T(8,128)(2,1)}, u32[]{:S(2)}) copy-start(bf16[256,256]{1,0:T(8,128)(2,1)} %param.10) | copy-start | bytes 393220
  11.6 76.0 %all-to-all-start = ((bf16[16,256,256]{2,1,0:T(8,128)(2,1)}), bf16[16,256,256]{2,1,0:T(8,128)(2,1)S(1)}, u32[]{:S(2)}, u32[]{:S(2)}) async-start(bf16[16,256,256]{2,1,0:T(8,128)(2,1)} %stack.2), calls=%async_computation | async-start | bytes 4194304 | tf_op jit(solution)/shard_map/all_to_all | solution.py:35
  21.9 149.1 %all-gather.6.cloned.1.call-start = ((), (), s32[]{:S(2)}) async-start(), calls=%async_computation.1 | async-start | bytes 2162688 | tf_op jit(solution)/shard_map/all_gather | solution.py:39
  22.7 219.1 %all-gather.10.cloned.1.call-start = ((), (), s32[]{:S(2)}) async-start(), calls=%async_computation.3 | async-start | bytes 4325376 | tf_op jit(solution)/shard_map/all_gather | solution.py:13
  22.8 0.6 copy-start.3
Sparse Core Ops, SparseCore 0:
  10.7 90.4 all-gather.7
  103.3 67.7 all-gather.5
  174.6 67.2 all-gather.9
